TPU v7x, 256 devices: a whole 4x4x8 slice. The times are simulated.
256 devices in a mesh: tensor: 2 (over core), row: 16 (over x, y), col: 8 (over z).
Axes of the slice: x: 4, y: 4, z: 8, core: 2. Of those that a mesh axis runs over, the one named last changes fastest.
Arguments:
- integral_tiles: bfloat16 [8192, 8, 4096], P(('tensor', 'row', 'col')), may hold values from -6 to 6
- tile_index: int32 [8192, 3], P(('tensor', 'row', 'col')), may hold values from 0 to 127, as said below
- virtual_coeff: bfloat16 [8192, 2048], P('col'), may hold values from -0.09375 to 0.09375
- occupied_coeff: bfloat16 [2048, 512], P('row'), may hold values from -0.125 to 0.125
Outputs:
- pair_tensor: bfloat16 [2048, 32, 512], P(('row', 'col'), 'tensor')
Inputs may be any that keep to these rules, and one draw needn't show every extreme that they name: `tile_index`: the tiles of the device at index (t, r, c) of tensor, row, col all have their nu block in c * 16 .. (c + 1) * 16 - 1, their auxiliary block below 4 and their mu block below 32. A tile's owner is (tensor index a // 2, row index m // 2) in the same col. Each device holds at most 2 tiles for any one owner; in every draw some owner gets exactly 2 tiles from every device of its col. Tiles with equal indices may occur and add up.
All inputs are finite; a program needn't handle non-finite values.
Results may differ from a plain program's by a relative error of at most 0.025.
Values may be sent and summed in bfloat16 or wider, within the bound.
No kernel may reach another device: no remote copies, remote signals or barrier semaphores. Data moves between devices by JAX's collectives and lax.ppermute only.
A program may use at most 128 MiB of HBM per device.

v0:
```python
import jax
import jax.numpy as jnp
from jax import lax
from jax.sharding import PartitionSpec as P

TB = 64
PB = 8
AB = 2
MB = 2
NBC = 16
CAP = 2
NV = 2048
NOCC = 512


def shards(integral_tiles, tile_index, virtual_coeff, occupied_coeff):
    tensor_at = lax.axis_index("tensor")
    row_at = lax.axis_index("row")
    col_at = lax.axis_index("col")
    tensor_count = lax.axis_size("tensor")
    row_count = lax.axis_size("row")
    col_count = lax.axis_size("col")
    held = integral_tiles.shape[0]
    aux_blocks = tensor_count * AB
    mu_blocks = row_count * MB
    quarters = tensor_count * 2
    qsize = TB // quarters
    assert row_count == 2 * PB and quarters * qsize == TB
    tiles = integral_tiles.reshape(held, PB, 2, tensor_count, qsize, TB)
    send = tiles.transpose(3, 1, 2, 0, 4, 5).reshape(tensor_count * row_count, held, qsize * TB)
    recv = lax.all_to_all(send, ("tensor", "row"), split_axis=0, concat_axis=0, tiled=True)
    recv = recv.reshape(tensor_count * row_count * held, qsize * TB)
    index = lax.all_gather(tile_index, ("tensor", "row"), axis=0, tiled=True)
    local_nu = index[:, 2] - col_at * NBC
    block = (index[:, 0] * NBC + local_nu) * mu_blocks + index[:, 1]
    blocks = aux_blocks * NBC * mu_blocks
    selector = (jnp.arange(blocks)[:, None] == block[None, :]).astype(jnp.bfloat16)
    dense = jnp.dot(selector, recv, preferred_element_type=jnp.float32).astype(jnp.bfloat16)
    dense = dense.reshape(aux_blocks, NBC, mu_blocks, qsize, TB)
    occ_all = lax.all_gather(occupied_coeff, "row", axis=0, tiled=True)
    quarter = 2 * (row_at % 2) + tensor_at
    occ_q = lax.dynamic_index_in_dim(
        occ_all.reshape(mu_blocks, quarters, qsize, NOCC), quarter, axis=1, keepdims=False
    )
    partial = jnp.einsum("anmuw,mui->anwi", dense, occ_q, preferred_element_type=jnp.float32)
    pair = lax.psum_scatter(partial.astype(jnp.bfloat16), "tensor", scatter_dimension=0, tiled=True)
    side = row_at % 2
    keep = lax.dynamic_index_in_dim(pair, side, axis=0, keepdims=False)
    give = lax.dynamic_index_in_dim(pair, 1 - side, axis=0, keepdims=False)
    got = lax.ppermute(give, "row", perm=[(i, i ^ 1) for i in range(row_count)])
    occ_done = (keep.astype(jnp.float32) + got.astype(jnp.float32)).astype(jnp.bfloat16)
    chunk = NV // (row_count * col_count)
    virt = virtual_coeff.reshape(NBC, TB, row_count, col_count, chunk)
    z = jnp.einsum("nwi,nwrcj->crji", occ_done, virt, preferred_element_type=jnp.float32)
    z = z.astype(jnp.bfloat16).reshape(col_count * row_count * chunk, NOCC)
    w = lax.psum_scatter(z, "col", scatter_dimension=0, tiled=True).reshape(row_count, chunk, NOCC)
    got_rows = lax.all_to_all(w, "row", split_axis=0, concat_axis=0, tiled=True)
    out = got_rows.reshape(PB, 2, chunk, NOCC).transpose(2, 1, 0, 3)
    return out.reshape(chunk, AB * PB, NOCC)


def solution(mesh):
    in_specs = (
        P(("tensor", "row", "col"), None, None),
        P(("tensor", "row", "col"), None),
        P("col", None),
        P("row", None),
    )
    out_specs = P(("row", "col"), "tensor", None)
    return jax.shard_map(shards, mesh=mesh, in_specs=in_specs, out_specs=out_specs, check_vma=False)
```

profile of v0, /device:TPU:32, one launch (start us, length us, event | category | flops | bytes accessed | tf_op | source)
XLA Modules:
  0.0 265.2 jit_solution(8073186442823905420)
XLA Ops:
  6.5 0.7 all-gather.3.cloned.1.call-update
  7.3 6.9 %reshape.57 = bf16[32,8,2,2,16,64]{5,4,3,2,1,0:T(8,128)(2,1)} reshape(bf16[32,8,4096]{2,1,0:T(8,128)(2,1)} %param.4) | data formatting | bytes 4194304 | tf_op jit(solution)/shard_map/reshape | solution.py:29
  14.2 5.3 %copy.42 = bf16[32,8,2,2,16,64]{5,4,0,2,1,3:T(8,128)(2,1)} copy(bf16[32,8,2,2,16,64]{5,4,3,2,1,0:T(8,128)(2,1)} %reshape.57) | data formatting | bytes 4194304 | tf_op jit(solution)/shard_map/reshape | solution.py:29
  19.5 6.5 %reshape.58 = bf16[32,32,1024]{2,1,0:T(8,128)(2,1)} reshape(bf16[2,8,2,32,16,64]{5,4,3,2,1,0:T(8,128)(2,1)} %bitcast.55) | data formatting | bytes 4194304 | tf_op jit(solution)/shard_map/reshape | solution.py:30
  26.0 7.3 %all-to-all-start = ((bf16[32,32,1024]{2,1,0:T(8,128)(2,1)}), bf16[32,32,1024]{2,1,0:T(8,128)(2,1)S(1)}, u32[]{:S(2)}, u32[]{:S(2)}) async-start(bf16[32,32,1024]{2,1,0:T(8,128)(2,1)} %reshape.58), calls=%async_computation | async-start | bytes 4194304 | tf_op jit(solution)/shard_map/all_to_all | solution.py:31
  33.4 0.0 reduce-scatter.3.cloned.1.call-start
  33.5 86.8 %all-gather = s32[32,32,3]{1,2,0:T(4,128)S(1)} all-gather(s32[1,32,3]{1,2,0:T(4,128)S(1)} %bitcast.62), channel_id=1, replica_groups=mesh['tensor'=2,'row'=16,'col'=8] {'tensor','row'}, dimensions={0}, use_global_device_ids=true | all-gather | bytes 12672 | tf_op jit(solution)/shard_map/all_gather | solution.py:33
  120.3 0.1 reshape.69
  120.4 6.0 %fusion.4 = bf16[2048,1024]{1,0:T(8,128)(2,1)} fusion(bf16[1024,1024]{1,0:T(8,128)(2,1)S(1)} %bitcast.57, s32[1024]{0:T(1024)S(1)} %bitcast.61), kind=kOutput, calls=%fused_computation.8 | convolution fusion | flops 4299161600 | bytes 6295552 | tf_op jit(solution)/shard_map/dot_general | solution.py:38
  126.4 11.6 %reshape.60 = bf16[4,16,32,16,64]{4,3,2,1,0:T(8,128)(2,1)} reshape(bf16[2048,1024]{1,0:T(8,128)(2,1)} %fusion.4) | data formatting | bytes 8388608 | tf_op jit(solution)/shard_map/reshape | solution.py:39
  138.0 7.8 %bitcast_convert_fusion = bf16[4,16,64,512]{3,2,1,0:T(8,128)(2,1)} fusion(bf16[4,16,32,16,64]{4,3,2,1,0:T(8,128)(2,1)} %reshape.60, bf16[32,4,16,512]{3,2,1,0:T(8,128)(2,1)} %bitcast.60, s32[]{:T(128)S(6)} %select_n.21), kind=kOutput, calls=%fused_computation | convolution fusion | flops 2149580800 | bytes 13107204 | tf_op jit(solution)/shard_map/anmuw,mui->anwi/dot_general | solution.py:45
  145.8 0.0 reduce-scatter.3.cloned.1.call-update
  145.8 0.0 reduce-scatter.5.cloned.1.call-start
  145.9 17.0 %reduce-scatter.3.cloned.1.call-done = bf16[2,16,64,512]{3,2,1,0:T(8,128)(2,1)} async-done(((bf16[4,16,64,512]{3,2,1,0:T(8,128)(2,1)}), bf16[2,16,64,512]{3,2,1,0:T(8,128)(2,1)}) %reduce-scatter.3.cloned.1.call-update) | async-done | bytes 2097168 | tf_op jit(solution)/shard_map/reduce_scatter | solution.py:46
  162.9 1.3 dynamic-slice_bitcast_fusion
  164.2 1.7 collective-permute-start
  165.9 6.4 %copy.25 = bf16[1024,2048]{0,1:T(8,128)(2,1)} copy(bf16[1024,2048]{1,0:T(8,128)(2,1)} %param.6) | data formatting | bytes 8388608 | tf_op args[2]
  172.3 11.8 %reshape.62 = bf16[16,64,16,8,16]{1,0,4,3,2:T(8,128)(2,1)} reshape(bf16[1024,2048]{0,1:T(8,128)(2,1)} %copy.25) | data formatting | bytes 8388608 | tf_op jit(solution)/shard_map/reshape | solution.py:53
  184.1 5.8 %collective-permute-done = bf16[16,64,512]{2,1,0:T(8,128)(2,1)} collective-permute-done((bf16[16,64,512]{2,1,0:T(8,128)(2,1)S(1)}, bf16[16,64,512]{2,1,0:T(8,128)(2,1)}, u32[]{:S(2)}, u32[]{:S(2)}) %collective-permute-start) | collective-permute-done | bytes 1048608 | tf_op jit(solution)/shard_map/ppermute | solution.py:50
  189.8 8.0 %fusion.8 = bf16[8,16,16,512]{3,2,0,1:T(8,128)(2,1)S(1)} fusion(bf16[16,64,16,8,16]{1,0,4,3,2:T(8,128)(2,1)} %reshape.62, bf16[16,64,512]{2,1,0:T(8,128)(2,1)} %collective-permute-done, bf16[2,16,64,512]{3,2,1,0:T(8,128)(2,1)S(1)} %copy-done, s32[]{:T(128)S(6)} %select_n.22), kind=kOutput, calls=%fused_computation.11 | convolution fusion | flops 2150629376 | bytes 8388612 | tf_op jit(solution)/shard_map/nwi,nwrcj->crji/dot_general | solution.py:54
  197.8 1.5 copy.27
  199.4 42.9 %reduce-scatter.5.cloned.1.call-done = bf16[256,512]{1,0:T(8,128)(2,1)} async-done(((bf16[2048,512]{1,0:T(8,128)(2,1)}), bf16[256,512]{1,0:T(8,128)(2,1)}) %reduce-scatter.5.cloned.1.call-update) | async-done | bytes 262160 | tf_op jit(solution)/shard_map/reduce_scatter | solution.py:56
  242.3 15.5 %all_to_all.10 = bf16[16,16,512]{2,1,0:T(8,128)(2,1)S(1)} all-to-all(bf16[16,16,512]{2,1,0:T(8,128)(2,1)} %bitcast.59), channel_id=1, replica_groups=mesh['tensor'=2,'row'=16,'col'=8] {'row'}, dimensions={0} | all-to-all | bytes 524288 | tf_op jit(solution)/shard_map/all_to_all | solution.py:57
  257.8 0.9 copy.43
  (10 shorter events, 0.1 us)
Async XLA Ops:
  6.5 131.5 %all-gather.3.cloned.1.call-start = ((), (), s32[]{:S(2)}) async-start(), calls=%async_computation.4 | async-start | bytes 2228224 | tf_op jit(solution)/shard_map/all_gather | solution.py:40
  19.5 13.9 %copy-start.1 = (s32[32,3]{0,1:T(4,128)S(1)}, s32[32,3]{0,1:T(4,128)}, u32[]{:S(2)}) copy-start(s32[32,3]{0,1:T(4,128)} %param.5) | copy-start | bytes 1156
  26.0 94.3 %all-to-all-start = ((bf16[32,32,1024]{2,1,0:T(8,128)(2,1)}), bf16[32,32,1024]{2,1,0:T(8,128)(2,1)S(1)}, u32[]{:S(2)}, u32[]{:S(2)}) async-start(bf16[32,32,1024]{2,1,0:T(8,128)(2,1)} %reshape.58), calls=%async_computation | async-start | bytes 4194304 | tf_op jit(solution)/shard_map/all_to_all | solution.py:31
  33.4 129.5 %reduce-scatter.3.cloned.1.call-start = ((), (), s32[]{:S(2)}) async-start(), calls=%async_computation.5 | async-start | bytes 6291456 | tf_op jit(solution)/shard_map/reduce_scatter | solution.py:46
  145.8 96.5 %reduce-scatter.5.cloned.1.call-start = ((), (), s32[]{:S(2)}) async-start(), calls=%async_computation.6 | async-start | bytes 2359296 | tf_op jit(solution)/shard_map/reduce_scatter | solution.py:56
  164.2 25.6 %collective-permute-start = (bf16[16,64,512]{2,1,0:T(8,128)(2,1)S(1)}, bf16[16,64,512]{2,1,0:T(8,128)(2,1)}, u32[]{:S(2)}, u32[]{:S(2)}) collective-permute-start(bf16[16,64,512]{2,1,0:T(8,128)(2,1)S(1)} %dynamic-slice_bitcast_fusion), channel_id=1, source_target_pairs={{0,8},{8,0},{16,24},{24,16},{32,40},{40,32},{48,56},{56,48},{64,72... | collective-permute-start | bytes 3145736 | tf_op jit(solution)/shard_map/ppermute | solution.py:50
  172.3 17.5 %copy-start = (bf16[2,16,64,512]{3,2,1,0:T(8,128)(2,1)S(1)}, bf16[2,16,64,512]{3,2,1,0:T(8,128)(2,1)}, u32[]{:S(2)}) copy-start(bf16[2,16,64,512]{3,2,1,0:T(8,128)(2,1)} %reduce-scatter.3.cloned.1.call-done) | copy-start | bytes 6291460
Sparse Core Ops, SparseCore 0:
  9.8 63.4 all-gather.2
  145.9 16.8 reduce-scatter.2
  199.5 42.7 reduce-scatter.4
where the time goes:
time: 266 us; the launch traced here: 265 us
  blocking collectives  102 us (38%)
  waiting for transfers between devices  66.4 us (25%)
  local copies, waits for them, and re-layouts  52.3 us (20%)
  matrix products  21.8 us (8%)
  between operations  13.2 us (5%)
  starting transfers between devices  9.15 us (3%)
    all_gather x1, blocking collectives, shards(): index = lax.all_gather(tile_index, ('tensor', 'row'), axis=0, tiled=True)  86.8 us
    reduce_scatter x1, waiting for transfers between devices, shards(): lax.psum_scatter(z, 'col', scatter_dimension=0, tiled=True)  42.9 us
    reduce_scatter x1, waiting for transfers between devices, shards(): lax.psum_scatter(partial.astype(jnp.bfloat16), 'tensor', scatter_dimensio...  17 us
    all_to_all x1, blocking collectives, shards(): got_rows = lax.all_to_all(w, 'row', split_axis=0, concat_axis=0, tiled=True)  15.5 us
    reshape x2, local copies, waits for them, and re-layouts, shards(): tiles = integral_tiles.reshape(held, PB, 2, tensor_count, qsize, TB)  12.3 us
    reshape x1, local copies, waits for them, and re-layouts, shards(): virt = virtual_coeff.reshape(NBC, TB, row_count, col_count, chunk)  11.8 us
    reshape x1, local copies, waits for them, and re-layouts, shards(): dense = dense.reshape(aux_blocks, NBC, mu_blocks, qsize, TB)  11.6 us
    dot_general x1, matrix products, shards(): jnp.einsum('nwi,nwrcj->crji', occ_done, virt, preferred_element_type=jnp....  7.97 us
  transfers between devices with their start and end apart: 5, of which 3 were waited for; matrix products, arithmetic and copies ran while one was open for 21% of the time, Pallas kernels for 0%

commit v1 on v0

--- a/solution.py
+++ b/solution.py
@@ -11,6 +11,11 @@
 CAP = 2
 NV = 2048
 NOCC = 512
+
+
+def swapped_in(x, name, dim):
+    repeated = jnp.stack([x] * lax.axis_size(name))
+    return jnp.concatenate(lax.all_to_all(repeated, name, 0, 0), axis=dim)
 
 
 def shards(integral_tiles, tile_index, virtual_coeff, occupied_coeff):
@@ -30,7 +35,7 @@
     send = tiles.transpose(3, 1, 2, 0, 4, 5).reshape(tensor_count * row_count, held, qsize * TB)
     recv = lax.all_to_all(send, ("tensor", "row"), split_axis=0, concat_axis=0, tiled=True)
     recv = recv.reshape(tensor_count * row_count * held, qsize * TB)
-    index = lax.all_gather(tile_index, ("tensor", "row"), axis=0, tiled=True)
+    index = swapped_in(tile_index, ("tensor", "row"), 0)
     local_nu = index[:, 2] - col_at * NBC
     block = (index[:, 0] * NBC + local_nu) * mu_blocks + index[:, 1]
     blocks = aux_blocks * NBC * mu_blocks

time: 266 us -> 225 us (0.85)
  blocking collectives: 102 us -> 15.2 us
  waiting for transfers between devices: 66.4 us -> 104 us
  starting transfers between devices: 9.15 us -> 16.5 us
    all_gather x1 -> x0, blocking collectives: 86.8 us -> none  [shards(): index = lax.all_gather(tile_index, ('tensor', 'row'), axis=0, tiled=True)]
    all_to_all x1, waiting for transfers between devices: 0.01 us -> 35.3 us  [shards(): lax.all_to_all(send, ('tensor', 'row'), split_axis=0, concat_axis=0, tile...]
    all_to_all x0 -> x1, starting transfers between devices: none -> 7.32 us  [swapped_in(): return jnp.concatenate(lax.all_to_all(repeated, name, 0, 0), axis=dim)]
    unnamed x6 -> x3, local copies, waits for them, and re-layouts: 6.47 us -> 6.4 us
  transfers between devices with their start and end apart: 5 -> 6, of which waited for: 3 -> 4; matrix products, arithmetic and copies ran while one was open for 21% -> 25% of each run, Pallas kernels for 0% -> 0%
where the time goes in v1:
time: 225 us; the launch traced here: 224 us
  waiting for transfers between devices  104 us (46%)
  local copies, waits for them, and re-layouts  53.7 us (24%)
  matrix products  21.8 us (10%)
  starting transfers between devices  16.5 us (7%)
  blocking collectives  15.2 us (7%)
  between operations  13.2 us (6%)
    reduce_scatter x1, waiting for transfers between devices, shards(): lax.psum_scatter(z, 'col', scatter_dimension=0, tiled=True)  43.2 us
    all_to_all x1, waiting for transfers between devices, shards(): lax.all_to_all(send, ('tensor', 'row'), split_axis=0, concat_axis=0, tile...  35.3 us
    reduce_scatter x1, waiting for transfers between devices, shards(): lax.psum_scatter(partial.astype(jnp.bfloat16), 'tensor', scatter_dimensio...  18.6 us
    all_to_all x1, blocking collectives, shards(): got_rows = lax.all_to_all(w, 'row', split_axis=0, concat_axis=0, tiled=True)  15.2 us
    reshape x2, local copies, waits for them, and re-layouts, shards(): tiles = integral_tiles.reshape(held, PB, 2, tensor_count, qsize, TB)  12.3 us
    reshape x1, local copies, waits for them, and re-layouts, shards(): virt = virtual_coeff.reshape(NBC, TB, row_count, col_count, chunk)  11.7 us
    reshape x1, local copies, waits for them, and re-layouts, shards(): dense = dense.reshape(aux_blocks, NBC, mu_blocks, qsize, TB)  11.6 us
    dot_general x1, matrix products, shards(): jnp.einsum('nwi,nwrcj->crji', occ_done, virt, preferred_element_type=jnp....  7.97 us
  transfers between devices with their start and end apart: 6, of which 4 were waited for; matrix products, arithmetic and copies ran while one was open for 25% of the time, Pallas kernels for 0%

profile of v1, /device:TPU:32, one launch (start us, length us, event | category | flops | bytes accessed | tf_op | source)
XLA Modules:
  0.0 223.9 jit_solution(2024560122701207661)
XLA Ops:
  6.5 0.7 all-gather.2.cloned.1.call-update
  7.3 1.3 stack.2
  8.6 7.3 %all-to-all-start = ((s32[32,32,3]{1,2,0:T(4,128)}), s32[32,32,3]{1,2,0:T(4,128)S(1)}, u32[]{:S(2)}, u32[]{:S(2)}) async-start(s32[32,32,3]{1,2,0:T(4,128)} %stack.2), calls=%async_computation | async-start | bytes 131072 | tf_op jit(solution)/shard_map/all_to_all | solution.py:18
  15.9 6.9 %reshape.63 = bf16[32,8,2,2,16,64]{5,4,3,2,1,0:T(8,128)(2,1)} reshape(bf16[32,8,4096]{2,1,0:T(8,128)(2,1)} %param.4) | data formatting | bytes 4194304 | tf_op jit(solution)/shard_map/reshape | solution.py:34
  22.8 5.4 %copy.47 = bf16[32,8,2,2,16,64]{5,4,0,2,1,3:T(8,128)(2,1)} copy(bf16[32,8,2,2,16,64]{5,4,3,2,1,0:T(8,128)(2,1)} %reshape.63) | data formatting | bytes 4194304 | tf_op jit(solution)/shard_map/reshape | solution.py:34
  28.2 6.5 %reshape.64 = bf16[32,32,1024]{2,1,0:T(8,128)(2,1)} reshape(bf16[2,8,2,32,16,64]{5,4,3,2,1,0:T(8,128)(2,1)} %bitcast.54) | data formatting | bytes 4194304 | tf_op jit(solution)/shard_map/reshape | solution.py:35
  34.7 7.4 %all-to-all-start.1 = ((bf16[32,32,1024]{2,1,0:T(8,128)(2,1)}), bf16[32,32,1024]{2,1,0:T(8,128)(2,1)S(1)}, u32[]{:S(2)}, u32[]{:S(2)}) async-start(bf16[32,32,1024]{2,1,0:T(8,128)(2,1)} %reshape.64), calls=%async_computation.1 | async-start | bytes 4194304 | tf_op jit(solution)/shard_map/all_to_all | solution.py:36
  42.1 0.0 reduce-scatter.3.cloned.1.call-start
  42.2 0.1 reshape.62
  42.3 35.3 %all-to-all-done.1 = bf16[32,32,1024]{2,1,0:T(8,128)(2,1)S(1)} async-done(((bf16[32,32,1024]{2,1,0:T(8,128)(2,1)}), bf16[32,32,1024]{2,1,0:T(8,128)(2,1)S(1)}, u32[]{:S(2)}, u32[]{:S(2)}) %all-to-all-start.1) | async-done | bytes 2097184 | tf_op jit(solution)/shard_map/all_to_all | solution.py:36
  77.7 6.0 %fusion.4 = bf16[2048,1024]{1,0:T(8,128)(2,1)} fusion(bf16[1024,1024]{1,0:T(8,128)(2,1)S(1)} %bitcast.56, s32[1024]{0:T(1024)S(1)} %bitcast.60), kind=kOutput, calls=%fused_computation.8 | convolution fusion | flops 4299161600 | bytes 6295552 | tf_op jit(solution)/shard_map/dot_general | solution.py:43
  83.7 11.6 %reshape.66 = bf16[4,16,32,16,64]{4,3,2,1,0:T(8,128)(2,1)} reshape(bf16[2048,1024]{1,0:T(8,128)(2,1)} %fusion.4) | data formatting | bytes 8388608 | tf_op jit(solution)/shard_map/reshape | solution.py:44
  95.3 7.8 %bitcast_convert_fusion = bf16[4,16,64,512]{3,2,1,0:T(8,128)(2,1)} fusion(bf16[4,16,32,16,64]{4,3,2,1,0:T(8,128)(2,1)} %reshape.66, bf16[32,4,16,512]{3,2,1,0:T(8,128)(2,1)} %bitcast.59, s32[]{:T(128)S(6)} %select_n.21), kind=kOutput, calls=%fused_computation | convolution fusion | flops 2149580800 | bytes 13107204 | tf_op jit(solution)/shard_map/anmuw,mui->anwi/dot_general | solution.py:50
  103.1 18.6 %reduce-scatter.3.cloned.1.call-done = bf16[2,16,64,512]{3,2,1,0:T(8,128)(2,1)} async-done(((bf16[4,16,64,512]{3,2,1,0:T(8,128)(2,1)}), bf16[2,16,64,512]{3,2,1,0:T(8,128)(2,1)}) %reduce-scatter.3.cloned.1.call-update) | async-done | bytes 2097168 | tf_op jit(solution)/shard_map/reduce_scatter | solution.py:51
  121.7 1.3 dynamic-slice_bitcast_fusion
  123.0 1.7 collective-permute-start
  124.8 6.4 %copy.30 = bf16[1024,2048]{0,1:T(8,128)(2,1)} copy(bf16[1024,2048]{1,0:T(8,128)(2,1)} %param.6) | data formatting | bytes 8388608 | tf_op args[2]
  131.2 11.7 %reshape.68 = bf16[16,64,16,8,16]{1,0,4,3,2:T(8,128)(2,1)} reshape(bf16[1024,2048]{0,1:T(8,128)(2,1)} %copy.30) | data formatting | bytes 8388608 | tf_op jit(solution)/shard_map/reshape | solution.py:58
  142.9 5.7 %collective-permute-done = bf16[16,64,512]{2,1,0:T(8,128)(2,1)} collective-permute-done((bf16[16,64,512]{2,1,0:T(8,128)(2,1)S(1)}, bf16[16,64,512]{2,1,0:T(8,128)(2,1)}, u32[]{:S(2)}, u32[]{:S(2)}) %collective-permute-start) | collective-permute-done | bytes 1048608 | tf_op jit(solution)/shard_map/ppermute | solution.py:55
  148.7 8.0 %fusion.8 = bf16[8,16,16,512]{3,2,0,1:T(8,128)(2,1)S(1)} fusion(bf16[16,64,16,8,16]{1,0,4,3,2:T(8,128)(2,1)} %reshape.68, bf16[16,64,512]{2,1,0:T(8,128)(2,1)} %collective-permute-done, bf16[2,16,64,512]{3,2,1,0:T(8,128)(2,1)S(1)} %copy-done, s32[]{:T(128)S(6)} %select_n.22), kind=kOutput, calls=%fused_computation.11 | convolution fusion | flops 2150629376 | bytes 8388612 | tf_op jit(solution)/shard_map/nwi,nwrcj->crji/dot_general | solution.py:59
  156.6 1.5 copy.32
  158.2 43.2 %reduce-scatter.5.cloned.1.call-done = bf16[256,512]{1,0:T(8,128)(2,1)} async-done(((bf16[2048,512]{1,0:T(8,128)(2,1)}), bf16[256,512]{1,0:T(8,128)(2,1)}) %reduce-scatter.5.cloned.1.call-update) | async-done | bytes 262160 | tf_op jit(solution)/shard_map/reduce_scatter | solution.py:61
  201.4 15.2 %all_to_all.15 = bf16[16,16,512]{2,1,0:T(8,128)(2,1)S(1)} all-to-all(bf16[16,16,512]{2,1,0:T(8,128)(2,1)} %bitcast.58), channel_id=1, replica_groups=mesh['tensor'=2,'row'=16,'col'=8] {'row'}, dimensions={0} | all-to-all | bytes 524288 | tf_op jit(solution)/shard_map/all_to_all | solution.py:62
  216.5 0.9 copy.48
  (10 shorter events, 0.1 us)
Async XLA Ops:
  6.5 88.7 %all-gather.2.cloned.1.call-start = ((), (), s32[]{:S(2)}) async-start(), calls=%async_computation.5 | async-start | bytes 2228224 | tf_op jit(solution)/shard_map/all_gather | solution.py:45
  8.6 26.1 %all-to-all-start = ((s32[32,32,3]{1,2,0:T(4,128)}), s32[32,32,3]{1,2,0:T(4,128)S(1)}, u32[]{:S(2)}, u32[]{:S(2)}) async-start(s32[32,32,3]{1,2,0:T(4,128)} %stack.2), calls=%async_computation | async-start | bytes 131072 | tf_op jit(solution)/shard_map/all_to_all | solution.py:18
  34.7 42.9 %all-to-all-start.1 = ((bf16[32,32,1024]{2,1,0:T(8,128)(2,1)}), bf16[32,32,1024]{2,1,0:T(8,128)(2,1)S(1)}, u32[]{:S(2)}, u32[]{:S(2)}) async-start(bf16[32,32,1024]{2,1,0:T(8,128)(2,1)} %reshape.64), calls=%async_computation.1 | async-start | bytes 4194304 | tf_op jit(solution)/shard_map/all_to_all | solution.py:36
  42.1 79.6 %reduce-scatter.3.cloned.1.call-start = ((), (), s32[]{:S(2)}) async-start(), calls=%async_computation.6 | async-start | bytes 6291456 | tf_op jit(solution)/shard_map/reduce_scatter | solution.py:51
  103.1 98.3 %reduce-scatter.5.cloned.1.call-start = ((), (), s32[]{:S(2)}) async-start(), calls=%async_computation.7 | async-start | bytes 2359296 | tf_op jit(solution)/shard_map/reduce_scatter | solution.py:61
  123.0 25.6 %collective-permute-start = (bf16[16,64,512]{2,1,0:T(8,128)(2,1)S(1)}, bf16[16,64,512]{2,1,0:T(8,128)(2,1)}, u32[]{:S(2)}, u32[]{:S(2)}) collective-permute-start(bf16[16,64,512]{2,1,0:T(8,128)(2,1)S(1)} %dynamic-slice_bitcast_fusion), channel_id=1, source_target_pairs={{0,8},{8,0},{16,24},{24,16},{32,40},{40,32},{48,56},{56,48},{64,72... | collective-permute-start | bytes 3145736 | tf_op jit(solution)/shard_map/ppermute | solution.py:55
  131.2 17.5 %copy-start = (bf16[2,16,64,512]{3,2,1,0:T(8,128)(2,1)S(1)}, bf16[2,16,64,512]{3,2,1,0:T(8,128)(2,1)}, u32[]{:S(2)}) copy-start(bf16[2,16,64,512]{3,2,1,0:T(8,128)(2,1)} %reduce-scatter.3.cloned.1.call-done) | copy-start | bytes 6291460
Sparse Core Ops, SparseCore 0:
  9.8 68.8 all-gather.1
  103.2 18.4 reduce-scatter.2
  158.3 43.0 reduce-scatter.4
